TPU v7x, 32 devices: a whole 2x2x4 slice. The times are simulated.
32 devices in a mesh: req: 8 (over z, x), kv: 4 (over y, core).
Axes of the slice: x: 2, y: 2, z: 4, core: 2. Of those that a mesh axis runs over, the one named last changes fastest.
Arguments:
- activations: bfloat16 [4992, 2048], P('req', 'kv'), may hold values from -6 to 6
- span_length: int32 [104], P('req'), may hold values from 1 to 48, as said below
- offsets: int32 [104], P('req'), may hold values from 64 to 8191
- decode_slot: int32 [104], P('req'), may hold values from 0 to 103, as said below
- attention_gain: float32 [2048], replicated, may hold values from 0.1 to 1.9
- query_weight: bfloat16 [2048, 2048], P(None, 'kv'), may hold values from -0.125 to 0.125
- key_projection_matrix: bfloat16 [2048, 1024], P(None, 'kv'), may hold values from -0.125 to 0.125
- value_projection_matrix: bfloat16 [2048, 1024], P(None, 'kv'), may hold values from -0.125 to 0.125
- output_weight: bfloat16 [2048, 2048], P('kv'), may hold values from -0.125 to 0.125
- feedforward_gain: float32 [2048], replicated, may hold values from 0.1 to 1.9
- gate_weight: bfloat16 [2048, 4096], P(None, 'kv'), may hold values from -0.125 to 0.125
- up_weight: bfloat16 [2048, 4096], P(None, 'kv'), may hold values from -0.125 to 0.125
- down_weight: bfloat16 [4096, 2048], P('kv'), may hold values from -0.09375 to 0.09375
- earlier_rotated_keys: bfloat16 [104, 64, 1024], P('req', 'kv'), may hold values from -300 to 300
- earlier_values: bfloat16 [104, 64, 1024], P('req', 'kv'), may hold values from -6 to 6
Outputs:
- layer_out: bfloat16 [4992, 2048], P('req', 'kv')
- decode_keys: bfloat16 [104, 64, 1024], P('req', None, 'kv')
- decode_values: bfloat16 [104, 64, 1024], P('req', None, 'kv')
Inputs may be any that keep to these rules, and one draw needn't show every extreme that they name: `span_length`: on some prefill device every request fills all 48 positions. `decode_slot`: each slot appears once; decode device d owns slots d * 13 to (d + 1) * 13 - 1; at most 2 requests of one prefill device go to one decode device; every prefill device p sends exactly 2 requests to decode device p + 1 (counted round); the differences of decode device minus prefill device, modulo the number of devices of req, form the same multiset on every prefill device.
All inputs are finite; a program needn't handle non-finite values.
Results may differ from a plain program's by a relative error of at most 0.012.
Values may be sent and summed in bfloat16 or wider, within the bound.
No kernel may reach another device: no remote copies, remote signals or barrier semaphores. Data moves between devices by JAX's collectives and lax.ppermute only.
A program may use at most 128 MiB of HBM per device.

v0:
```python
import math
import jax
import jax.numpy as jnp
from jax import lax
from jax.sharding import Mesh
from jax.sharding import PartitionSpec as P

HEAD_WIDTH = 256
CORES = 2
rope_base = 1000042.0
epsilon = 1e-05


def rotate_pairs(tensor, position):
    half_size = tensor.shape[-1] // 2
    steps_float = jnp.arange(half_size, dtype=jnp.float32)
    inverse = jnp.exp(steps_float * (-2.0 * math.log(rope_base) / tensor.shape[-1]))
    angles = position[:, :, None] * inverse[None, None, :]
    cosine = jnp.cos(angles)[:, :, None, :]
    sine_part = jnp.sin(angles)[:, :, None, :]
    first_half = tensor[..., :half_size]
    second = tensor[..., half_size:]
    return jnp.concatenate(
        [first_half * cosine - second * sine_part, second * cosine + first_half * sine_part],
        axis=-1,
    )


def allowed_keys(span_length, span_size, past_size):
    key_pos = jnp.arange(past_size + span_size, dtype=jnp.int32) - past_size
    query_pos = jnp.arange(span_size, dtype=jnp.int32)
    causal = key_pos[None, :] <= query_pos[:, None]
    live_keys = key_pos[None, None, :] < span_length[:, None, None]
    return (key_pos[None, None, :] < 0) | causal[None, :, :] & live_keys


def gather_features(share):
    chips = lax.axis_size("kvy")
    rows, width = share.shape
    pair = lax.all_gather(share, "kvy", axis=1, tiled=True)
    whole = lax.all_gather(pair, "core", axis=1, tiled=True)
    whole = whole.reshape(rows, CORES, chips, width).transpose(0, 2, 1, 3)
    return whole.reshape(rows, CORES * chips * width)


def swap_blocks(matrix):
    chips = lax.axis_size("kvy")
    rows, cols = matrix.shape
    width = cols // (CORES * chips)
    return matrix.reshape(rows, chips, CORES, width).transpose(0, 2, 1, 3).reshape(rows, cols)


def scatter_features(partial):
    on_chip = lax.psum_scatter(partial, "core", scatter_dimension=1, tiled=True)
    return lax.psum_scatter(on_chip, "kvy", scatter_dimension=1, tiled=True)


def row_scale(values, gain_share):
    square_sum = lax.psum(jnp.sum(values * values, axis=-1, keepdims=True), ("kvy", "core"))
    width = values.shape[-1] * lax.axis_size("kvy") * CORES
    return values * lax.rsqrt(square_sum / width + epsilon) * gain_share


def local(
    activations,
    span_length,
    offsets,
    decode_slot,
    attention_gain,
    query_weight,
    key_projection_matrix,
    value_projection_matrix,
    output_weight,
    feedforward_gain,
    gate_weight,
    up_weight,
    down_weight,
    earlier_rotated_keys,
    earlier_values,
):
    req_count = lax.axis_size("req")
    chips = lax.axis_size("kvy")
    kv_count = chips * CORES
    kv_index = lax.axis_index("kvy") * CORES + lax.axis_index("core")
    req_index = lax.axis_index("req")
    request_list = span_length.shape[0]
    total_rows, width_share = activations.shape
    span_size = total_rows // request_list
    local_kv = key_projection_matrix.shape[1] // HEAD_WIDTH
    local_q = query_weight.shape[1] // HEAD_WIDTH
    query_groups = local_q // local_kv
    past_share = earlier_rotated_keys.shape[1]
    stacked = jnp.stack([earlier_rotated_keys, earlier_values])
    stacked = stacked.reshape(2, request_list, past_share, kv_count, local_kv * HEAD_WIDTH)
    stacked = stacked.transpose(0, 3, 1, 2, 4)
    arrived = lax.all_to_all(stacked, ("kvy", "core"), split_axis=1, concat_axis=1, tiled=True)
    head_kv = arrived.transpose(0, 2, 1, 3, 4).reshape(
        2, request_list, kv_count * past_share, local_kv * HEAD_WIDTH
    )
    past_size = head_kv.shape[2]
    capacity = max(2, (request_list + req_count - 1) // req_count)
    order_ids = jnp.arange(request_list, dtype=jnp.int32)
    earlier = order_ids[None, :] < order_ids[:, None]
    own_dest = decode_slot // request_list
    same_dest = own_dest[:, None] == own_dest[None, :]
    own_rank = jnp.sum((same_dest & earlier).astype(jnp.int32), axis=1)
    buffer_place = own_dest * capacity + own_rank
    buffer_ids = jnp.arange(req_count * capacity, dtype=jnp.int32)
    matches = buffer_place[None, :] == buffer_ids[:, None]
    picked = jnp.sum(jnp.where(matches, order_ids[None, :], 0), axis=1)
    filled = jnp.any(matches, axis=1)
    packed = jnp.take(head_kv, picked, axis=1)
    packed = jnp.where(filled[None, :, None, None], packed, jnp.zeros((), packed.dtype))
    packed = packed.reshape((2, req_count, capacity) + packed.shape[2:])
    packed_slots = jnp.where(filled, jnp.take(decode_slot, picked), -1).reshape(req_count, capacity)
    landed = lax.all_to_all(packed, "req", split_axis=1, concat_axis=1, tiled=True)
    landed_slots = lax.all_to_all(packed_slots, "req", split_axis=0, concat_axis=0, tiled=True)
    wanted = req_index * request_list + order_ids
    slot_hits = landed_slots.reshape(1, -1) == wanted[:, None]
    entry_ids = jnp.arange(req_count * capacity, dtype=jnp.int32)
    slot_position = jnp.sum(jnp.where(slot_hits, entry_ids[None, :], 0), axis=1)
    landed = landed.reshape((2, req_count * capacity) + landed.shape[3:])
    decode_kv = jnp.take(landed, slot_position, axis=1)
    x_whole = gather_features(activations)
    x_float = x_whole.astype(jnp.float32)
    square_sum = jnp.sum(x_float * x_float, axis=-1, keepdims=True)
    normalized_input = (
        x_float * lax.rsqrt(square_sum / x_float.shape[-1] + epsilon) * attention_gain
    ).astype(jnp.bfloat16)
    position = (
        offsets[:, None].astype(jnp.float32) + jnp.arange(span_size, dtype=jnp.float32)[None, :]
    )
    query_rows = jnp.dot(
        normalized_input, query_weight, preferred_element_type=jnp.float32
    ).reshape(request_list, span_size, local_q, HEAD_WIDTH)
    query_rows = rotate_pairs(query_rows, position).astype(jnp.bfloat16)
    fresh_keys = jnp.dot(
        normalized_input, key_projection_matrix, preferred_element_type=jnp.float32
    ).reshape(request_list, span_size, local_kv, HEAD_WIDTH)
    fresh_keys = rotate_pairs(fresh_keys, position).astype(jnp.bfloat16)
    fresh_values = (
        jnp.dot(normalized_input, value_projection_matrix, preferred_element_type=jnp.float32)
        .astype(jnp.bfloat16)
        .reshape(request_list, span_size, local_kv, HEAD_WIDTH)
    )
    combined_keys = jnp.concatenate(
        [head_kv[0].reshape(request_list, past_size, local_kv, HEAD_WIDTH), fresh_keys], axis=1
    )
    combined_values = jnp.concatenate(
        [head_kv[1].reshape(request_list, past_size, local_kv, HEAD_WIDTH), fresh_values], axis=1
    )
    grouped_queries = query_rows.reshape(
        request_list, span_size, local_kv, query_groups, HEAD_WIDTH
    )
    scores = jnp.einsum(
        "rckgd,rskd->rkgcs", grouped_queries, combined_keys, preferred_element_type=jnp.float32
    ) / math.sqrt(HEAD_WIDTH)
    allowed = allowed_keys(span_length, span_size, past_size)[:, None, None, :, :]
    scores = jnp.where(allowed, scores, -jnp.inf)
    weights = jax.nn.softmax(scores, axis=-1).astype(jnp.bfloat16)
    mixed_heads = jnp.einsum(
        "rkgcs,rskd->rckgd", weights, combined_values, preferred_element_type=jnp.float32
    )
    mixed_heads = mixed_heads.astype(jnp.bfloat16).reshape(total_rows, local_q * HEAD_WIDTH)
    head_part = jnp.dot(mixed_heads, swap_blocks(output_weight), preferred_element_type=jnp.float32)
    head_share = scatter_features(head_part)
    residual_share = activations.astype(jnp.float32) + head_share
    gain_share = lax.dynamic_slice_in_dim(feedforward_gain, kv_index * width_share, width_share)
    normed_share = row_scale(residual_share, gain_share).astype(jnp.bfloat16)
    normed_two = gather_features(normed_share)
    gate_proj = jnp.dot(normed_two, gate_weight, preferred_element_type=jnp.float32)
    upward = jnp.dot(normed_two, up_weight, preferred_element_type=jnp.float32)
    hidden = (jax.nn.silu(gate_proj) * upward).astype(jnp.bfloat16)
    mlp_share = scatter_features(
        jnp.dot(hidden, swap_blocks(down_weight), preferred_element_type=jnp.float32)
    )
    live_rows = (jnp.arange(span_size, dtype=jnp.int32)[None, :] < span_length[:, None]).reshape(
        total_rows
    )
    layer_out = jnp.where(live_rows[:, None], residual_share + mlp_share, 0.0).astype(jnp.bfloat16)
    return (layer_out, decode_kv[0], decode_kv[1])


def solution(mesh):
    req_size, kv_size = mesh.devices.shape
    split_mesh = Mesh(
        mesh.devices.reshape(req_size, kv_size // CORES, CORES), ("req", "kvy", "core")
    )
    kv = ("kvy", "core")
    return jax.shard_map(
        local,
        mesh=split_mesh,
        in_specs=(
            P("req", kv),
            P("req"),
            P("req"),
            P("req"),
            P(),
            P(None, kv),
            P(None, kv),
            P(None, kv),
            P(kv, None),
            P(),
            P(None, kv),
            P(None, kv),
            P(kv, None),
            P("req", kv, None),
            P("req", kv, None),
        ),
        out_specs=(P("req", kv), P("req", None, kv), P("req", None, kv)),
        check_vma=False,
    )
```

profile of v0, /device:TPU:0, one launch (start us, length us, event | category | flops | bytes accessed | tf_op | source)
XLA Modules:
  0.0 338.3 jit_solution(16456305696777216266)
XLA Ops:
  8.0 28.2 %all-gather.5.cloned.1.call-done = bf16[624,1024]{1,0:T(8,128)(2,1)} async-done(((bf16[624,512]{1,0:T(8,128)(2,1)}), bf16[624,1024]{1,0:T(8,128)(2,1)}) %all-gather.5.cloned.1.call-update) | async-done | bytes 1277968 | tf_op jit(solution)/shard_map/all_gather | solution.py:40
  42.3 4.4 %all-to-all-start = ((bf16[2,4,13,16,256]{4,3,2,0,1:T(8,128)(2,1)}), bf16[2,4,13,16,256]{4,3,2,0,1:T(8,128)(2,1)}, u32[]{:S(2)}, u32[]{:S(2)}) async-start(bf16[2,4,13,16,256]{4,3,2,0,1:T(8,128)(2,1)} %copy.111), calls=%async_computation | async-start | bytes 1703936 | tf_op jit(solution)/shard_map/all_to_all | solution.py:96
  46.8 2.5 copy.132
  49.3 2.9 copy.120
  55.1 4.0 %all-to-all-done = bf16[2,4,13,16,256]{4,3,2,0,1:T(8,128)(2,1)} async-done(((bf16[2,4,13,16,256]{4,3,2,0,1:T(8,128)(2,1)}), bf16[2,4,13,16,256]{4,3,2,0,1:T(8,128)(2,1)}, u32[]{:S(2)}, u32[]{:S(2)}) %all-to-all-start) | async-done | bytes 852000 | tf_op jit(solution)/shard_map/all_to_all | solution.py:96
  61.5 4.8 %copy.113 = f32[624,2048]{0,1:T(8,128)} copy(bf16[624,2048]{1,0:T(8,128)(2,1)} %all-gather.7.cloned.1.call-done) | data formatting | bytes 7667712 | tf_op jit(solution)/shard_map/convert_element_type | solution.py:125
  66.3 3.0 multiply_reduce_fusion
  69.3 8.9 %copy.115 = f32[624,2,2,512]{3,2,1,0:T(2,128)} copy(f32[624,2,2,512]{0,3,1,2:T(8,128)} %bitcast.105) | data formatting | bytes 10223616 | tf_op jit(solution)/shard_map/convert_element_type | solution.py:125
  78.2 5.1 %copy.114 = f32[624,2,2,512]{0,3,2,1:T(8,128)} copy(f32[624,2,2,512]{0,3,1,2:T(8,128)} %bitcast.106) | data formatting | bytes 10223616 | tf_op jit(solution)/shard_map/convert_element_type | solution.py:125
  83.4 5.8 %copy.116 = f32[624,2,2,512]{3,0,1,2:T(8,128)} copy(f32[624,2,2,512]{0,3,2,1:T(8,128)} %bitcast.107) | data formatting | bytes 10223616 | tf_op jit(solution)/shard_map/convert_element_type | solution.py:125
  89.3 3.0 fusion.2
  92.3 4.1 %copy.117 = bf16[624,2,2,512]{3,2,1,0:T(2,128)(2,1)} copy(bf16[624,2,2,512]{3,0,2,1:T(8,128)(2,1)S(1)} %fusion.2) | data formatting | bytes 5111808 | tf_op jit(solution)/shard_map/convert_element_type | solution.py:129
  96.4 7.1 %reshape.453 = bf16[13,48,2048,1]{2,1,0,3:T(8,128)(2,1)} reshape(bf16[624,2,2,512]{3,2,1,0:T(2,128)(2,1)} %copy.117) | data formatting | bytes 5111808 | tf_op jit(solution)/shard_map/convert_element_type | solution.py:129
  103.4 8.0 %reshape.424 = f32[13,48,2048]{2,1,0:T(8,128)} reshape(f32[624,2,2,512]{3,2,1,0:T(2,128)} %copy.115) | data formatting | bytes 10223616 | tf_op jit(solution)/shard_map/convert_element_type | solution.py:125
  111.4 3.3 fusion.9
  116.4 3.2 fusion.1
  125.7 3.8 %fusion.44 = f32[624,2048]{1,0:T(8,128)} fusion(bf16[624,512]{1,0:T(8,128)(2,1)S(1)} %bitcast.117, bf16[512,2048]{0,1:T(8,128)(2,1)S(1)} %bitcast.112), kind=kOutput, calls=%fused_computation.103 | convolution fusion | flops 1308622848 | bytes 7847936 | tf_op jit(solution)/shard_map/dot_general | solution.py:165
  129.6 13.2 %reduce-scatter.5.cloned.1.call-done = f32[624,1024]{1,0:T(8,128)} async-done(((f32[624,2048]{1,0:T(8,128)}), f32[624,1024]{1,0:T(8,128)}) %reduce-scatter.5.cloned.1.call-update) | async-done | bytes 2555920 | tf_op jit(solution)/shard_map/reduce_scatter | solution.py:54
  143.6 39.5 %reduce-scatter.7.cloned.1.call-done = f32[624,512]{1,0:T(8,128)} async-done(((f32[624,1024]{1,0:T(8,128)}), f32[624,512]{1,0:T(8,128)}) %reduce-scatter.7.cloned.1.call-update) | async-done | bytes 1277968 | tf_op jit(solution)/shard_map/reduce_scatter | solution.py:55
  184.7 5.8 %psum.7 = f32[624,1]{0,1:T(1,128)S(1)} all-reduce(f32[624,1]{0,1:T(1,128)S(1)} %broadcast_in_dim.128), channel_id=1, replica_groups=mesh['req'=8,'kvy'=2,'core'=2] {'kvy','core'}, use_global_device_ids=true, to_apply=%region_6.7 | all-reduce | flops 624 | bytes 4992 | tf_op jit(solution)/shard_map/psum | solution.py:59
  191.6 25.1 %all-gather.9.cloned.1.call-done = bf16[624,1024]{1,0:T(8,128)(2,1)} async-done(((bf16[624,512]{1,0:T(8,128)(2,1)}), bf16[624,1024]{1,0:T(8,128)(2,1)}) %all-gather.9.cloned.1.call-update) | async-done | bytes 1277968 | tf_op jit(solution)/shard_map/all_gather | solution.py:40
  216.8 6.6 %copy.123 = bf16[1024,2048]{0,1:T(8,128)(2,1)} copy(bf16[1024,2048]{1,0:T(8,128)(2,1)} %param.27) | data formatting | bytes 8388608 | tf_op args[12]
  223.4 5.1 %copy.124 = bf16[1024,2,2,512]{0,3,2,1:T(8,128)(2,1)} copy(bf16[1024,2,2,512]{0,3,1,2:T(8,128)(2,1)} %bitcast.108) | data formatting | bytes 8388608 | tf_op jit(solution)/shard_map/transpose | solution.py:50
  229.4 7.1 %reshape.417 = bf16[624,2,2,512]{3,2,1,0:T(2,128)(2,1)} reshape(bf16[624,2048]{1,0:T(8,128)(2,1)} %all-gather.11.cloned.1.call-done) | data formatting | bytes 5111808 | tf_op jit(solution)/shard_map/reshape | solution.py:42
  236.5 7.5 %copy.122 = bf16[624,2,2,512]{0,3,1,2:T(8,128)(2,1)} copy(bf16[624,2,2,512]{3,2,1,0:T(2,128)(2,1)} %reshape.417) | data formatting | bytes 5111808 | tf_op jit(solution)/shard_map/reshape | solution.py:42
  244.0 7.3 %fusion.45 = f32[624,1024]{1,0:T(8,128)} fusion(bf16[624,2048]{0,1:T(8,128)(2,1)} %bitcast.118, bf16[2048,1024]{1,0:T(8,128)(2,1)} %param.25), kind=kOutput, calls=%fused_computation.104 | convolution fusion | flops 2617245696 | bytes 9306112 | tf_op jit(solution)/shard_map/dot_general | solution.py:171
  251.4 13.0 %fusion.19 = f32[624,2048]{1,0:T(8,128)} fusion(bf16[1024,2048]{0,1:T(8,128)(2,1)} %bitcast.115, f32[624,1024]{1,0:T(8,128)} %fusion.45, bf16[624,2048]{0,1:T(8,128)(2,1)} %bitcast.119, bf16[2048,1024]{1,0:T(8,128)(2,1)} %param.26), kind=kOutput, calls=%fused_computation.39 | convolution fusion | flops 5238325248 | bytes 18612224 | tf_op jit(solution)/shard_map/dot_general | solution.py:175
  264.5 14.3 %reduce-scatter.9.cloned.1.call-done = f32[624,1024]{1,0:T(8,128)} async-done(((f32[624,2048]{1,0:T(8,128)}), f32[624,1024]{1,0:T(8,128)}) %reduce-scatter.9.cloned.1.call-update) | async-done | bytes 2555920 | tf_op jit(solution)/shard_map/reduce_scatter | solution.py:54
  280.8 5.8 %all-to-all-start.1 = ((s32[8,1,2]{2,1,0:T(1,128)}), s32[8,1,2]{2,1,0:T(1,128)S(1)}, u32[]{:S(2)}, u32[]{:S(2)}) async-start(s32[8,1,2]{2,1,0:T(1,128)} %bitcast.38), calls=%async_computation.5 | async-start | bytes 8192 | tf_op jit(solution)/shard_map/all_to_all | solution.py:117
  293.0 4.2 %all-to-all-start.2 = ((bf16[2,8,2,64,256]{4,3,2,0,1:T(8,128)(2,1)}), bf16[2,8,2,64,256]{4,3,2,0,1:T(8,128)(2,1)S(1)}, u32[]{:S(2)}, u32[]{:S(2)}) async-start(bf16[2,8,2,64,256]{4,3,2,0,1:T(8,128)(2,1)} %copy.127), calls=%async_computation.6 | async-start | bytes 2097152 | tf_op jit(solution)/shard_map/all_to_all | solution.py:116
  298.9 24.1 %all-to-all-done.2 = bf16[2,8,2,64,256]{4,3,2,0,1:T(8,128)(2,1)S(1)} async-done(((bf16[2,8,2,64,256]{4,3,2,0,1:T(8,128)(2,1)}), bf16[2,8,2,64,256]{4,3,2,0,1:T(8,128)(2,1)S(1)}, u32[]{:S(2)}, u32[]{:S(2)}) %all-to-all-start.2) | async-done | bytes 1048608 | tf_op jit(solution)/shard_map/all_to_all | solution.py:116
  324.1 2.7 gather_fusion.2
  (118 shorter events, 40.4 us)
Async XLA Ops:
  7.2 104.3 %copy-start = (bf16[2048,256]{1,0:T(8,128)(2,1)S(1)}, bf16[2048,256]{1,0:T(8,128)(2,1)}, u32[]{:S(2)}) copy-start(bf16[2048,256]{1,0:T(8,128)(2,1)} %param.21) | copy-start | bytes 3145732
  7.2 31.1 %copy-start.11 = (bf16[13,16,1024]{2,1,0:T(8,128)(2,1)S(1)}, bf16[13,16,1024]{2,1,0:T(8,128)(2,1)}, u32[]{:S(2)}) copy-start(bf16[13,16,1024]{2,1,0:T(8,128)(2,1)} %param.28) | copy-start | bytes 1277956
  7.2 29.0 %all-gather.5.cloned.1.call-start = ((), (), s32[]{:S(2)}) async-start(), calls=%async_computation.7 | async-start | bytes 1916928 | tf_op jit(solution)/shard_map/all_gather | solution.py:40
  7.9 53.6 %all-gather.7.cloned.1.call-start = ((), (), s32[]{:S(2)}) async-start(), calls=%async_computation.8 | async-start | bytes 3833856 | tf_op jit(solution)/shard_map/all_gather | solution.py:41
  39.4 7.4 %copy-start.12 = (f32[2048]{0:T(1024)S(1)}, f32[2048]{0:T(1024)}, u32[]{:S(2)}) copy-start(f32[2048]{0:T(1024)} %param.19) | copy-start | bytes 24580
  39.4 7.5 %copy-start.9 = (bf16[2048,512]{1,0:T(8,128)(2,1)S(1)}, bf16[2048,512]{1,0:T(8,128)(2,1)}, u32[]{:S(2)}) copy-start(bf16[2048,512]{1,0:T(8,128)(2,1)} %param.20) | copy-start | bytes 6291460
  42.3 7.0 %copy-start.15 = (s32[13]{0:T(128)S(1)}, s32[13]{0:T(128)}, u32[]{:S(2)}) copy-start(s32[13]{0:T(128)} %param.17) | copy-start | bytes 160
  42.3 16.8 %all-to-all-start = ((bf16[2,4,13,16,256]{4,3,2,0,1:T(8,128)(2,1)}), bf16[2,4,13,16,256]{4,3,2,0,1:T(8,128)(2,1)}, u32[]{:S(2)}, u32[]{:S(2)}) async-start(bf16[2,4,13,16,256]{4,3,2,0,1:T(8,128)(2,1)} %copy.111), calls=%async_computation | async-start | bytes 1703936 | tf_op jit(solution)/shard_map/all_to_all | solution.py:96
  46.7 96.0 %reduce-scatter.5.cloned.1.call-start = ((), (), s32[]{:S(2)}) async-start(), calls=%async_computation.9 | async-start | bytes 7667712 | tf_op jit(solution)/shard_map/reduce_scatter | solution.py:54
  52.2 1.6 copy-start.13
  60.4 1.0 copy-start.5
  116.3 3.3 copy-start.8
  116.4 3.9 %copy-start.10 = (bf16[512,2048]{1,0:T(8,128)(2,1)S(1)}, bf16[512,2048]{1,0:T(8,128)(2,1)}, u32[]{:S(2)}) copy-start(bf16[512,2048]{1,0:T(8,128)(2,1)} %copy.132) | copy-start | bytes 6291460
  122.0 1.2 copy-start.14
  124.1 1.6 copy-start.7
  129.5 53.6 %copy-start.4 = (bf16[624,512]{1,0:T(8,128)(2,1)S(1)}, bf16[624,512]{1,0:T(8,128)(2,1)}, u32[]{:S(2)}) copy-start(bf16[624,512]{1,0:T(8,128)(2,1)} %param.15) | copy-start | bytes 1916932
  129.5 53.5 %reduce-scatter.7.cloned.1.call-start = ((), (), s32[]{:S(2)}) async-start(), calls=%async_computation.10 | async-start | bytes 3833856 | tf_op jit(solution)/shard_map/reduce_scatter | solution.py:55
  142.8 74.0 %all-gather.9.cloned.1.call-start = ((), (), s32[]{:S(2)}) async-start(), calls=%async_computation.11 | async-start | bytes 1916928 | tf_op jit(solution)/shard_map/all_gather | solution.py:40
  183.1 7.5 %copy-start.3 = (f32[624,512]{1,0:T(8,128)S(1)}, f32[624,512]{1,0:T(8,128)}, u32[]{:S(2)}) copy-start(f32[624,512]{1,0:T(8,128)} %reduce-scatter.7.cloned.1.call-done) | copy-start | bytes 3833860
  191.6 37.8 %all-gather.11.cloned.1.call-start = ((), (), s32[]{:S(2)}) async-start(), calls=%async_computation.12 | async-start | bytes 3833856 | tf_op jit(solution)/shard_map/all_gather | solution.py:41
  216.8 62.0 %reduce-scatter.9.cloned.1.call-start = ((), (), s32[]{:S(2)}) async-start(), calls=%async_computation.13 | async-start | bytes 7667712 | tf_op jit(solution)/shard_map/reduce_scatter | solution.py:54
  264.4 14.4 %copy-start.2 = (s32[13]{0:T(128)S(1)}, s32[13]{0:T(128)}, u32[]{:S(2)}) copy-start(s32[13]{0:T(128)} %param.18) | copy-start | bytes 160
  264.4 22.4 %copy-start.6 = (bf16[2,4,13,16,256]{4,3,1,2,0:T(8,128)(2,1)S(1)}, bf16[2,4,13,16,256]{4,3,1,2,0:T(8,128)(2,1)}, u32[]{:S(2)}) copy-start(bf16[2,4,13,16,256]{4,3,1,2,0:T(8,128)(2,1)} %copy-done.5) | copy-start | bytes 2555908
  264.4 64.7 %reduce-scatter.11.cloned.1.call-start = ((), (), s32[]{:S(2)}) async-start(), calls=%async_computation.14 | async-start | bytes 3833856 | tf_op jit(solution)/shard_map/reduce_scatter | solution.py:55
  280.8 12.2 %all-to-all-start.1 = ((s32[8,1,2]{2,1,0:T(1,128)}), s32[8,1,2]{2,1,0:T(1,128)S(1)}, u32[]{:S(2)}, u32[]{:S(2)}) async-start(s32[8,1,2]{2,1,0:T(1,128)} %bitcast.38), calls=%async_computation.5 | async-start | bytes 8192 | tf_op jit(solution)/shard_map/all_to_all | solution.py:117
  293.0 29.9 %all-to-all-start.2 = ((bf16[2,8,2,64,256]{4,3,2,0,1:T(8,128)(2,1)}), bf16[2,8,2,64,256]{4,3,2,0,1:T(8,128)(2,1)S(1)}, u32[]{:S(2)}, u32[]{:S(2)}) async-start(bf16[2,8,2,64,256]{4,3,2,0,1:T(8,128)(2,1)} %copy.127), calls=%async_computation.6 | async-start | bytes 2097152 | tf_op jit(solution)/shard_map/all_to_all | solution.py:116
  326.8 4.7 %copy-start.1 = (bf16[2048,256]{1,0:T(8,128)(2,1)S(1)}, bf16[2048,256]{1,0:T(8,128)(2,1)}, u32[]{:S(2)}) copy-start(bf16[2048,256]{1,0:T(8,128)(2,1)} %param.21) | copy-start | bytes 3145732
Sparse Core Ops, SparseCore 0:
  9.6 26.5 all-gather.4
  37.7 11.5 all-gather.6
  129.6 13.0 reduce-scatter.4
  144.9 38.0 reduce-scatter.6
  191.7 24.9 all-gather.8
  218.1 11.2 all-gather.10
  264.5 14.2 reduce-scatter.8
  281.1 38.1 reduce-scatter.10
where the time goes:
time: 340 us; the launch traced here: 338 us
  waiting for transfers between devices  152 us (45%)
  local copies, waits for them, and re-layouts  97.2 us (29%)
  matrix products  30.8 us (9%)
  other arithmetic  23.4 us (7%)
  starting transfers between devices  14.7 us (4%)
  between operations  14.5 us (4%)
  blocking collectives  5.76 us (2%)
    all_gather x2, waiting for transfers between devices, gather_features(): pair = lax.all_gather(share, 'kvy', axis=1, tiled=True)  53.3 us
    reduce_scatter x2, waiting for transfers between devices, scatter_features(): return lax.psum_scatter(on_chip, 'kvy', scatter_dimension=1, tiled=True)  39.5 us
    convert_element_type x5, local copies, waits for them, and re-layouts, local(): x_float = x_whole.astype(jnp.float32)  32.7 us
    reduce_scatter x2, waiting for transfers between devices, scatter_features(): on_chip = lax.psum_scatter(partial, 'core', scatter_dimension=1, tiled=True)  27.5 us
    all_to_all x1, waiting for transfers between devices, local(): lax.all_to_all(packed, 'req', split_axis=1, concat_axis=1, tiled=True)  24.1 us
    reshape x2, local copies, waits for them, and re-layouts, gather_features(): whole = whole.reshape(rows, CORES, chips, width).transpose(0, 2, 1, 3)  14.6 us
    dot_general x1, matrix products, local(): jnp.dot(hidden, swap_blocks(down_weight), preferred_element_type=jnp.floa...  13 us
    unnamed x35, local copies, waits for them, and re-layouts  12 us
  transfers between devices with their start and end apart: 11, of which 9 were waited for; matrix products, arithmetic and copies ran while one was open for 13% of the time, Pallas kernels for 0%

commit v1 on v0

--- a/solution.py
+++ b/solution.py
@@ -9,6 +9,17 @@
 CORES = 2
 rope_base = 1000042.0
 epsilon = 1e-05
+
+
+def cut_along(x, dim, peers):
+    before, after = (x.shape[:dim], x.shape[dim + 1 :])
+    return jnp.moveaxis(x.reshape(*before, peers, -1, *after), dim, 0)
+
+
+def in_order(blocks, dim):
+    blocks = jnp.moveaxis(blocks, 0, dim)
+    shape = blocks.shape
+    return blocks.reshape(*shape[:dim], shape[dim] * shape[dim + 1], *shape[dim + 2 :])
 
 
 def rotate_pairs(tensor, position):
@@ -114,7 +125,15 @@
     packed = packed.reshape((2, req_count, capacity) + packed.shape[2:])
     packed_slots = jnp.where(filled, jnp.take(decode_slot, picked), -1).reshape(req_count, capacity)
     landed = lax.all_to_all(packed, "req", split_axis=1, concat_axis=1, tiled=True)
-    landed_slots = lax.all_to_all(packed_slots, "req", split_axis=0, concat_axis=0, tiled=True)
+    size, index = (lax.axis_size("req"), lax.axis_index("req"))
+    blocks = cut_along(packed_slots, 0, size)
+    whole_2 = blocks
+    for step in range(1, size):
+        target, source = ((index + step) % size, (index - step) % size)
+        sent = lax.dynamic_index_in_dim(blocks, target, 0)
+        other = lax.ppermute(sent, "req", [(i, (i + step) % size) for i in range(size)])
+        whole_2 = lax.dynamic_update_slice_in_dim(whole_2, other, source, axis=0)
+    landed_slots = in_order(whole_2, 0)
     wanted = req_index * request_list + order_ids
     slot_hits = landed_slots.reshape(1, -1) == wanted[:, None]
     entry_ids = jnp.arange(req_count * capacity, dtype=jnp.int32)

time: 340 us -> 334 us (0.982)
  waiting for transfers between devices: 152 us -> 142 us
  starting transfers between devices: 14.7 us -> 20.3 us
    all_to_all x1, waiting for transfers between devices: 24.1 us -> 0.01 us  [local(): lax.all_to_all(packed, 'req', split_axis=1, concat_axis=1, tiled=True)]
    ppermute x0 -> x7, waiting for transfers between devices: none -> 16.1 us  [local(): lax.ppermute(sent, 'req', [(i, (i + step) % size) for i in range(size)])]
    ppermute x0 -> x7, starting transfers between devices: none -> 9.79 us  [local(): lax.ppermute(sent, 'req', [(i, (i + step) % size) for i in range(size)])]
    all_to_all x1 -> x0, starting transfers between devices: 5.82 us -> none  [local(): lax.all_to_all(packed_slots, 'req', split_axis=0, concat_axis=0, tiled=True)]
  transfers between devices with their start and end apart: 11 -> 17, of which waited for: 9 -> 9; matrix products, arithmetic and copies ran while one was open for 13% -> 12% of each run, Pallas kernels for 0% -> 0%
where the time goes in v1:
time: 334 us; the launch traced here: 332 us
  waiting for transfers between devices  142 us (43%)
  local copies, waits for them, and re-layouts  95.8 us (29%)
  matrix products  30.8 us (9%)
  other arithmetic  22.2 us (7%)
  starting transfers between devices  20.3 us (6%)
  between operations  14.6 us (4%)
  blocking collectives  5.76 us (2%)
    all_gather x2, waiting for transfers between devices, gather_features(): pair = lax.all_gather(share, 'kvy', axis=1, tiled=True)  53.3 us
    reduce_scatter x2, waiting for transfers between devices, scatter_features(): return lax.psum_scatter(on_chip, 'kvy', scatter_dimension=1, tiled=True)  39.5 us
    convert_element_type x5, local copies, waits for them, and re-layouts, local(): x_float = x_whole.astype(jnp.float32)  32.7 us
    reduce_scatter x2, waiting for transfers between devices, scatter_features(): on_chip = lax.psum_scatter(partial, 'core', scatter_dimension=1, tiled=True)  27.5 us
    ppermute x7, waiting for transfers between devices, local(): lax.ppermute(sent, 'req', [(i, (i + step) % size) for i in range(size)])  16.1 us
    reshape x2, local copies, waits for them, and re-layouts, gather_features(): whole = whole.reshape(rows, CORES, chips, width).transpose(0, 2, 1, 3)  14.6 us
    dot_general x1, matrix products, local(): jnp.dot(hidden, swap_blocks(down_weight), preferred_element_type=jnp.floa...  13 us
    unnamed x35, local copies, waits for them, and re-layouts  12.1 us
  transfers between devices with their start and end apart: 17, of which 9 were waited for; matrix products, arithmetic and copies ran while one was open for 12% of the time, Pallas kernels for 0%

profile of v1, /device:TPU:0, one launch (start us, length us, event | category | flops | bytes accessed | tf_op | source)
XLA Modules:
  0.0 331.5 jit_solution(13441504756632972524)
XLA Ops:
  8.0 28.2 %all-gather.5.cloned.1.call-done = bf16[624,1024]{1,0:T(8,128)(2,1)} async-done(((bf16[624,512]{1,0:T(8,128)(2,1)}), bf16[624,1024]{1,0:T(8,128)(2,1)}) %all-gather.5.cloned.1.call-update) | async-done | bytes 1277968 | tf_op jit(solution)/shard_map/all_gather | solution.py:51
  42.4 4.4 %all-to-all-start = ((bf16[2,4,13,16,256]{4,3,2,0,1:T(8,128)(2,1)}), bf16[2,4,13,16,256]{4,3,2,0,1:T(8,128)(2,1)}, u32[]{:S(2)}, u32[]{:S(2)}) async-start(bf16[2,4,13,16,256]{4,3,2,0,1:T(8,128)(2,1)} %copy.107), calls=%async_computation | async-start | bytes 1703936 | tf_op jit(solution)/shard_map/all_to_all | solution.py:107
  46.8 2.5 copy.127
  49.3 2.9 copy.116
  55.1 4.1 %all-to-all-done = bf16[2,4,13,16,256]{4,3,2,0,1:T(8,128)(2,1)} async-done(((bf16[2,4,13,16,256]{4,3,2,0,1:T(8,128)(2,1)}), bf16[2,4,13,16,256]{4,3,2,0,1:T(8,128)(2,1)}, u32[]{:S(2)}, u32[]{:S(2)}) %all-to-all-start) | async-done | bytes 852000 | tf_op jit(solution)/shard_map/all_to_all | solution.py:107
  61.5 4.9 %copy.109 = f32[624,2048]{0,1:T(8,128)} copy(bf16[624,2048]{1,0:T(8,128)(2,1)} %all-gather.7.cloned.1.call-done) | data formatting | bytes 7667712 | tf_op jit(solution)/shard_map/convert_element_type | solution.py:144
  66.4 3.0 multiply_reduce_fusion
  69.3 8.9 %copy.111 = f32[624,2,2,512]{3,2,1,0:T(2,128)} copy(f32[624,2,2,512]{0,3,1,2:T(8,128)} %bitcast.106) | data formatting | bytes 10223616 | tf_op jit(solution)/shard_map/convert_element_type | solution.py:144
  78.2 5.1 %copy.110 = f32[624,2,2,512]{0,3,2,1:T(8,128)} copy(f32[624,2,2,512]{0,3,1,2:T(8,128)} %bitcast.107) | data formatting | bytes 10223616 | tf_op jit(solution)/shard_map/convert_element_type | solution.py:144
  83.4 5.8 %copy.112 = f32[624,2,2,512]{3,0,1,2:T(8,128)} copy(f32[624,2,2,512]{0,3,2,1:T(8,128)} %bitcast.108) | data formatting | bytes 10223616 | tf_op jit(solution)/shard_map/convert_element_type | solution.py:144
  89.3 3.0 fusion.2
  92.3 4.1 %copy.113 = bf16[624,2,2,512]{3,2,1,0:T(2,128)(2,1)} copy(bf16[624,2,2,512]{3,0,2,1:T(8,128)(2,1)S(1)} %fusion.2) | data formatting | bytes 5111808 | tf_op jit(solution)/shard_map/convert_element_type | solution.py:148
  96.4 7.1 %reshape.445 = bf16[13,48,2048,1]{2,1,0,3:T(8,128)(2,1)} reshape(bf16[624,2,2,512]{3,2,1,0:T(2,128)(2,1)} %copy.113) | data formatting | bytes 5111808 | tf_op jit(solution)/shard_map/convert_element_type | solution.py:148
  103.5 8.0 %reshape.416 = f32[13,48,2048]{2,1,0:T(8,128)} reshape(f32[624,2,2,512]{3,2,1,0:T(2,128)} %copy.111) | data formatting | bytes 10223616 | tf_op jit(solution)/shard_map/convert_element_type | solution.py:144
  111.4 3.3 %fusion.9 = f32[13,48,1,256]{3,1,0,2:T(8,128)S(1)} fusion(f32[13,48,2048]{2,1,0:T(8,128)} %reshape.416, f32[2048]{0:T(1024)S(1)} %copy-done.12, f32[13,48]{1,0:T(8,128)S(1)} %rsqrt.17, bf16[2048,256]{1,0:T(8,128)(2,1)S(1)} %copy-done), kind=kOutput, calls=%fused_computation.22 | convolution fusion | flops 658145280 | bytes 6810048 | tf_op jit(solution)/shard_map/dot_general | solution.py:156
  116.4 3.2 fusion.1
  125.7 3.8 %fusion.44 = f32[624,2048]{1,0:T(8,128)} fusion(bf16[624,512]{1,0:T(8,128)(2,1)S(1)} %bitcast.118, bf16[512,2048]{0,1:T(8,128)(2,1)S(1)} %bitcast.113), kind=kOutput, calls=%fused_computation.110 | convolution fusion | flops 1308622848 | bytes 7847936 | tf_op jit(solution)/shard_map/dot_general | solution.py:184
  129.6 13.2 %reduce-scatter.5.cloned.1.call-done = f32[624,1024]{1,0:T(8,128)} async-done(((f32[624,2048]{1,0:T(8,128)}), f32[624,1024]{1,0:T(8,128)}) %reduce-scatter.5.cloned.1.call-update) | async-done | bytes 2555920 | tf_op jit(solution)/shard_map/reduce_scatter | solution.py:65
  143.6 39.5 %reduce-scatter.7.cloned.1.call-done = f32[624,512]{1,0:T(8,128)} async-done(((f32[624,1024]{1,0:T(8,128)}), f32[624,512]{1,0:T(8,128)}) %reduce-scatter.7.cloned.1.call-update) | async-done | bytes 1277968 | tf_op jit(solution)/shard_map/reduce_scatter | solution.py:66
  184.7 5.8 %psum.7 = f32[624,1]{0,1:T(1,128)S(1)} all-reduce(f32[624,1]{0,1:T(1,128)S(1)} %broadcast_in_dim.128), channel_id=1, replica_groups=mesh['req'=8,'kvy'=2,'core'=2] {'kvy','core'}, use_global_device_ids=true, to_apply=%region_6.7 | all-reduce | flops 624 | bytes 4992 | tf_op jit(solution)/shard_map/psum | solution.py:70
  191.6 25.1 %all-gather.9.cloned.1.call-done = bf16[624,1024]{1,0:T(8,128)(2,1)} async-done(((bf16[624,512]{1,0:T(8,128)(2,1)}), bf16[624,1024]{1,0:T(8,128)(2,1)}) %all-gather.9.cloned.1.call-update) | async-done | bytes 1277968 | tf_op jit(solution)/shard_map/all_gather | solution.py:51
  216.8 6.6 %copy.119 = bf16[1024,2048]{0,1:T(8,128)(2,1)} copy(bf16[1024,2048]{1,0:T(8,128)(2,1)} %param.27) | data formatting | bytes 8388608 | tf_op args[12]
  223.4 5.1 %copy.120 = bf16[1024,2,2,512]{0,3,2,1:T(8,128)(2,1)} copy(bf16[1024,2,2,512]{0,3,1,2:T(8,128)(2,1)} %bitcast.109) | data formatting | bytes 8388608 | tf_op jit(solution)/shard_map/transpose | solution.py:61
  229.4 7.1 %reshape.409 = bf16[624,2,2,512]{3,2,1,0:T(2,128)(2,1)} reshape(bf16[624,2048]{1,0:T(8,128)(2,1)} %all-gather.11.cloned.1.call-done) | data formatting | bytes 5111808 | tf_op jit(solution)/shard_map/reshape | solution.py:53
  236.5 7.5 %copy.118 = bf16[624,2,2,512]{0,3,1,2:T(8,128)(2,1)} copy(bf16[624,2,2,512]{3,2,1,0:T(2,128)(2,1)} %reshape.409) | data formatting | bytes 5111808 | tf_op jit(solution)/shard_map/reshape | solution.py:53
  244.0 7.3 %fusion.45 = f32[624,1024]{1,0:T(8,128)} fusion(bf16[624,2048]{0,1:T(8,128)(2,1)} %bitcast.119, bf16[2048,1024]{1,0:T(8,128)(2,1)} %param.25), kind=kOutput, calls=%fused_computation.111 | convolution fusion | flops 2617245696 | bytes 9306112 | tf_op jit(solution)/shard_map/dot_general | solution.py:190
  251.3 13.0 %fusion.19 = f32[624,2048]{1,0:T(8,128)} fusion(bf16[1024,2048]{0,1:T(8,128)(2,1)} %bitcast.116, f32[624,1024]{1,0:T(8,128)} %fusion.45, bf16[624,2048]{0,1:T(8,128)(2,1)} %bitcast.120, bf16[2048,1024]{1,0:T(8,128)(2,1)} %param.26), kind=kOutput, calls=%fused_computation.39 | convolution fusion | flops 5238325248 | bytes 18612224 | tf_op jit(solution)/shard_map/dot_general | solution.py:194
  264.4 14.3 %reduce-scatter.9.cloned.1.call-done = f32[624,1024]{1,0:T(8,128)} async-done(((f32[624,2048]{1,0:T(8,128)}), f32[624,1024]{1,0:T(8,128)}) %reduce-scatter.9.cloned.1.call-update) | async-done | bytes 2555920 | tf_op jit(solution)/shard_map/reduce_scatter | solution.py:65
  283.7 5.8 %all-to-all-start.1 = ((bf16[2,8,2,64,256]{4,3,2,0,1:T(8,128)(2,1)}), bf16[2,8,2,64,256]{4,3,2,0,1:T(8,128)(2,1)}, u32[]{:S(2)}, u32[]{:S(2)}) async-start(bf16[2,8,2,64,256]{4,3,2,0,1:T(8,128)(2,1)} %copy.122), calls=%async_computation.5 | async-start | bytes 2097152 | tf_op jit(solution)/shard_map/all_to_all | solution.py:127
  297.8 2.4 collective-permute-start.4
  300.4 11.6 %collective-permute-done = s32[1,1,2]{2,0,1:T(1,128)S(1)} collective-permute-done((s32[1,1,2]{2,0,1:T(1,128)S(1)}, s32[1,1,2]{2,0,1:T(1,128)S(1)}, u32[]{:S(2)}, u32[]{:S(2)}) %collective-permute-start) | collective-permute-done | bytes 40 | tf_op jit(solution)/shard_map/ppermute | solution.py:134
  312.1 4.5 %collective-permute-done.2 = s32[1,1,2]{2,0,1:T(1,128)S(1)} collective-permute-done((s32[1,1,2]{2,0,1:T(1,128)S(1)}, s32[1,1,2]{2,0,1:T(1,128)S(1)}, u32[]{:S(2)}, u32[]{:S(2)}) %collective-permute-start.2) | collective-permute-done | bytes 40 | tf_op jit(solution)/shard_map/ppermute | solution.py:134
  (136 shorter events, 46.1 us)
Async XLA Ops:
  7.2 104.3 %copy-start = (bf16[2048,256]{1,0:T(8,128)(2,1)S(1)}, bf16[2048,256]{1,0:T(8,128)(2,1)}, u32[]{:S(2)}) copy-start(bf16[2048,256]{1,0:T(8,128)(2,1)} %param.21) | copy-start | bytes 3145732
  7.2 31.1 %copy-start.11 = (bf16[13,16,1024]{2,1,0:T(8,128)(2,1)S(1)}, bf16[13,16,1024]{2,1,0:T(8,128)(2,1)}, u32[]{:S(2)}) copy-start(bf16[13,16,1024]{2,1,0:T(8,128)(2,1)} %param.28) | copy-start | bytes 1277956
  7.2 29.0 %all-gather.5.cloned.1.call-start = ((), (), s32[]{:S(2)}) async-start(), calls=%async_computation.6 | async-start | bytes 1916928 | tf_op jit(solution)/shard_map/all_gather | solution.py:51
  7.9 53.6 %all-gather.7.cloned.1.call-start = ((), (), s32[]{:S(2)}) async-start(), calls=%async_computation.7 | async-start | bytes 3833856 | tf_op jit(solution)/shard_map/all_gather | solution.py:52
  39.4 7.4 %copy-start.12 = (f32[2048]{0:T(1024)S(1)}, f32[2048]{0:T(1024)}, u32[]{:S(2)}) copy-start(f32[2048]{0:T(1024)} %param.19) | copy-start | bytes 24580
  39.4 7.4 %copy-start.9 = (bf16[2048,512]{1,0:T(8,128)(2,1)S(1)}, bf16[2048,512]{1,0:T(8,128)(2,1)}, u32[]{:S(2)}) copy-start(bf16[2048,512]{1,0:T(8,128)(2,1)} %param.20) | copy-start | bytes 6291460
  42.4 6.9 %copy-start.15 = (s32[13]{0:T(128)S(1)}, s32[13]{0:T(128)}, u32[]{:S(2)}) copy-start(s32[13]{0:T(128)} %param.17) | copy-start | bytes 160
  42.4 16.8 %all-to-all-start = ((bf16[2,4,13,16,256]{4,3,2,0,1:T(8,128)(2,1)}), bf16[2,4,13,16,256]{4,3,2,0,1:T(8,128)(2,1)}, u32[]{:S(2)}, u32[]{:S(2)}) async-start(bf16[2,4,13,16,256]{4,3,2,0,1:T(8,128)(2,1)} %copy.107), calls=%async_computation | async-start | bytes 1703936 | tf_op jit(solution)/shard_map/all_to_all | solution.py:107
  46.7 96.0 %reduce-scatter.5.cloned.1.call-start = ((), (), s32[]{:S(2)}) async-start(), calls=%async_computation.8 | async-start | bytes 7667712 | tf_op jit(solution)/shard_map/reduce_scatter | solution.py:65
  52.2 1.6 copy-start.13
  116.3 3.3 copy-start.8
  116.4 3.9 %copy-start.10 = (bf16[512,2048]{1,0:T(8,128)(2,1)S(1)}, bf16[512,2048]{1,0:T(8,128)(2,1)}, u32[]{:S(2)}) copy-start(bf16[512,2048]{1,0:T(8,128)(2,1)} %copy.127) | copy-start | bytes 6291460
  122.0 1.2 copy-start.14
  124.1 1.6 copy-start.7
  129.5 53.6 %copy-start.4 = (bf16[624,512]{1,0:T(8,128)(2,1)S(1)}, bf16[624,512]{1,0:T(8,128)(2,1)}, u32[]{:S(2)}) copy-start(bf16[624,512]{1,0:T(8,128)(2,1)} %param.15) | copy-start | bytes 1916932
  129.5 53.5 %reduce-scatter.7.cloned.1.call-start = ((), (), s32[]{:S(2)}) async-start(), calls=%async_computation.9 | async-start | bytes 3833856 | tf_op jit(solution)/shard_map/reduce_scatter | solution.py:66
  142.7 74.0 %all-gather.9.cloned.1.call-start = ((), (), s32[]{:S(2)}) async-start(), calls=%async_computation.10 | async-start | bytes 1916928 | tf_op jit(solution)/shard_map/all_gather | solution.py:51
  183.1 7.5 %copy-start.3 = (f32[624,512]{1,0:T(8,128)S(1)}, f32[624,512]{1,0:T(8,128)}, u32[]{:S(2)}) copy-start(f32[624,512]{1,0:T(8,128)} %reduce-scatter.7.cloned.1.call-done) | copy-start | bytes 3833860
  191.6 37.8 %all-gather.11.cloned.1.call-start = ((), (), s32[]{:S(2)}) async-start(), calls=%async_computation.11 | async-start | bytes 3833856 | tf_op jit(solution)/shard_map/all_gather | solution.py:52
  216.7 62.0 %reduce-scatter.9.cloned.1.call-start = ((), (), s32[]{:S(2)}) async-start(), calls=%async_computation.12 | async-start | bytes 7667712 | tf_op jit(solution)/shard_map/reduce_scatter | solution.py:65
  264.4 14.4 %copy-start.2 = (s32[13]{0:T(128)S(1)}, s32[13]{0:T(128)}, u32[]{:S(2)}) copy-start(s32[13]{0:T(128)} %param.18) | copy-start | bytes 160
  264.4 15.1 %copy-start.6 = (bf16[2,4,13,16,256]{4,3,1,2,0:T(8,128)(2,1)S(1)}, bf16[2,4,13,16,256]{4,3,1,2,0:T(8,128)(2,1)}, u32[]{:S(2)}) copy-start(bf16[2,4,13,16,256]{4,3,1,2,0:T(8,128)(2,1)} %copy-done.5) | copy-start | bytes 2555908
  264.4 57.9 %reduce-scatter.11.cloned.1.call-start = ((), (), s32[]{:S(2)}) async-start(), calls=%async_computation.13 | async-start | bytes 3833856 | tf_op jit(solution)/shard_map/reduce_scatter | solution.py:66
  283.7 33.4 %all-to-all-start.1 = ((bf16[2,8,2,64,256]{4,3,2,0,1:T(8,128)(2,1)}), bf16[2,8,2,64,256]{4,3,2,0,1:T(8,128)(2,1)}, u32[]{:S(2)}, u32[]{:S(2)}) async-start(bf16[2,8,2,64,256]{4,3,2,0,1:T(8,128)(2,1)} %copy.122), calls=%async_computation.5 | async-start | bytes 2097152 | tf_op jit(solution)/shard_map/all_to_all | solution.py:127
  290.5 21.5 %collective-permute-start = (s32[1,1,2]{2,0,1:T(1,128)S(1)}, s32[1,1,2]{2,0,1:T(1,128)S(1)}, u32[]{:S(2)}, u32[]{:S(2)}) collective-permute-start(s32[1,1,2]{2,0,1:T(1,128)S(1)} %get-tuple-element.21), channel_id=1, source_target_pairs={{0,4},{4,8},{8,12},{12,16},{16,20},{20,24},{24,28},{28,0},{1,5},{5... | collective-permute-start | bytes 32 | tf_op jit(solution)/shard_map/ppermute | solution.py:134
  292.5 19.5 %collective-permute-start.1 = (s32[1,1,2]{2,0,1:T(1,128)S(1)}, s32[1,1,2]{2,0,1:T(1,128)S(1)}, u32[]{:S(2)}, u32[]{:S(2)}) collective-permute-start(s32[1,1,2]{2,0,1:T(1,128)S(1)} %get-tuple-element.20), channel_id=1, source_target_pairs={{0,8},{4,12},{8,16},{12,20},{16,24},{20,28},{24,0},{28,4},{1,9},{5... | collective-permute-start | bytes 32 | tf_op jit(solution)/shard_map/ppermute | solution.py:134
  294.0 22.6 %collective-permute-start.2 = (s32[1,1,2]{2,0,1:T(1,128)S(1)}, s32[1,1,2]{2,0,1:T(1,128)S(1)}, u32[]{:S(2)}, u32[]{:S(2)}) collective-permute-start(s32[1,1,2]{2,0,1:T(1,128)S(1)} %get-tuple-element.19), channel_id=1, source_target_pairs={{0,12},{4,16},{8,20},{12,24},{16,28},{20,0},{24,4},{28,8},{1,13},{... | collective-permute-start | bytes 32 | tf_op jit(solution)/shard_map/ppermute | solution.py:134
  296.4 20.2 %collective-permute-start.3 = (s32[1,1,2]{2,0,1:T(1,128)S(1)}, s32[1,1,2]{2,0,1:T(1,128)S(1)}, u32[]{:S(2)}, u32[]{:S(2)}) collective-permute-start(s32[1,1,2]{2,0,1:T(1,128)S(1)} %get-tuple-element.18), channel_id=1, source_target_pairs={{0,16},{4,20},{8,24},{12,28},{16,0},{20,4},{24,8},{28,12},{1,17},{... | collective-permute-start | bytes 32 | tf_op jit(solution)/shard_map/ppermute | solution.py:134
  297.8 18.8 %collective-permute-start.4 = (s32[1,1,2]{2,0,1:T(1,128)S(1)}, s32[1,1,2]{2,0,1:T(1,128)S(1)}, u32[]{:S(2)}, u32[]{:S(2)}) collective-permute-start(s32[1,1,2]{2,0,1:T(1,128)S(1)} %get-tuple-element.17), channel_id=1, source_target_pairs={{0,20},{4,24},{8,28},{12,0},{16,4},{20,8},{24,12},{28,16},{1,21},{... | collective-permute-start | bytes 32 | tf_op jit(solution)/shard_map/ppermute | solution.py:134
  312.0 4.7 %collective-permute-start.5 = (s32[1,1,2]{2,0,1:T(1,128)S(1)}, s32[1,1,2]{2,0,1:T(1,128)S(1)}, u32[]{:S(2)}, u32[]{:S(2)}) collective-permute-start(s32[1,1,2]{2,0,1:T(1,128)S(1)} %get-tuple-element.16), channel_id=1, source_target_pairs={{0,24},{4,28},{8,0},{12,4},{16,8},{20,12},{24,16},{28,20},{1,25},{... | collective-permute-start | bytes 32 | tf_op jit(solution)/shard_map/ppermute | solution.py:134
  312.0 4.7 %collective-permute-start.6 = (s32[1,1,2]{2,0,1:T(1,128)S(1)}, s32[1,1,2]{2,0,1:T(1,128)S(1)}, u32[]{:S(2)}, u32[]{:S(2)}) collective-permute-start(s32[1,1,2]{2,0,1:T(1,128)S(1)} %get-tuple-element.15), channel_id=1, source_target_pairs={{0,28},{4,0},{8,4},{12,8},{16,12},{20,16},{24,20},{28,24},{1,29},{... | collective-permute-start | bytes 32 | tf_op jit(solution)/shard_map/ppermute | solution.py:134
  320.0 4.7 %copy-start.1 = (bf16[2048,256]{1,0:T(8,128)(2,1)S(1)}, bf16[2048,256]{1,0:T(8,128)(2,1)}, u32[]{:S(2)}) copy-start(bf16[2048,256]{1,0:T(8,128)(2,1)} %param.21) | copy-start | bytes 3145732
  (1 other events, 1.0 us)
Sparse Core Ops, SparseCore 0:
  9.6 26.5 all-gather.4
  37.7 11.5 all-gather.6
  129.6 13.0 reduce-scatter.4
  144.9 38.0 reduce-scatter.6
  191.7 24.9 all-gather.8
  218.1 11.2 all-gather.10
  264.5 14.2 reduce-scatter.8
  281.1 38.1 reduce-scatter.10
